TPU v7x, 512 devices: a whole 4x8x8 slice. The times are simulated.
512 devices in a mesh: dom: 128 (over z, y, core), feat: 4 (over x).
Axes of the slice: x: 4, y: 8, z: 8, core: 2. Of those that a mesh axis runs over, the one named last changes fastest.
Arguments:
- node_feats: bfloat16 [256, 262144], P('feat', 'dom'), may hold values from -6 to 6
- weight: bfloat16 [256, 256], P(None, 'feat'), may hold values from -0.375 to 0.375
- bias_vec: bfloat16 [256], P('feat'), may hold values from -3 to 3
- adj_tiles: bfloat16 [12288, 128, 128], P('dom'), may hold values from -0.25 to 0.25
- tile_row: int32 [12288], P('dom'), may hold values from 0 to 15, as said below
- tile_col: int32 [12288], P('dom'), may hold values from 0 to 143, as said below
- tile_count: int32 [128], P('dom'), may hold values from 58 to 96
- send_block: int32 [16384], P('dom'), may hold values from 0 to 15, as said below
- cotangent: bfloat16 [256, 262144], P('feat', 'dom'), may hold values from -6 to 6
Outputs:
- activations: bfloat16 [256, 262144], P('feat', 'dom')
- grad_input: bfloat16 [256, 262144], P('feat', 'dom')
- grad_weight: float32 [256, 256], P(None, 'feat')
- grad_bias: float32 [256], P('feat')
Inputs may be any that keep to these rules, and one draw needn't show every extreme that they name: `tile_row`: entries past a partition's tile_count are padding, of the same range. `tile_col`: among a partition's valid entries, each peer's halo slot 16 + q is named at most once, and a partition's own slot never. `send_block`: entry q * 128 + p is the local block that partition q sends to partition p; it is defined for every pair.
All inputs are finite; a program needn't handle non-finite values.
Results may differ from a plain program's by a relative error of at most 0.0064.
Values may be sent and summed in bfloat16 or wider, within the bound.
No kernel may reach another device: no remote copies, remote signals or barrier semaphores. Data moves between devices by JAX's collectives and lax.ppermute only.
A program may use at most 64 MiB of HBM per device.

v0:
```python
import math
import jax
import jax.numpy as jnp
from jax import lax
from jax.sharding import PartitionSpec as P


def smooth_gate(values):
    return jax.nn.gelu(values, approximate=True)


def per_device(
    node_feats, weight, bias_vec, adj_tiles, tile_row, tile_col, tile_count, send_block, cotangent
):
    feat_rows, node_rows = node_feats.shape
    tile_slots = adj_tiles.shape[0]
    tile_size = adj_tiles.shape[1]
    blocks = node_rows // tile_size
    domains = lax.axis_size("dom")
    whole = lax.all_gather(node_feats, "feat", axis=0, tiled=True)
    hidden = lax.dot_general(
        weight, whole, (((0,), (0,)), ((), ())), preferred_element_type=jnp.float32
    ).astype(jnp.bfloat16)
    hid_blocks = hidden.reshape(feat_rows, blocks, tile_size)
    outgoing = jnp.take(hid_blocks, send_block, axis=1)
    incoming = lax.all_to_all(outgoing, "dom", split_axis=1, concat_axis=1, tiled=True)
    sources = jnp.concatenate([hid_blocks, incoming], axis=1)
    live_tiles = jnp.arange(tile_slots) < tile_count[0]
    live_float = live_tiles.astype(jnp.float32)
    row_place = (tile_row[:, None] == jnp.arange(blocks)[None, :]).astype(jnp.float32) * live_float[
        :, None
    ]
    picked = jnp.take(sources, tile_col, axis=1)
    products = jnp.einsum("otb,tab->ota", picked, adj_tiles, preferred_element_type=jnp.float32)
    summed = jnp.einsum(
        "ota,tr->ora", products, row_place, precision=lax.Precision.HIGHEST
    ).reshape(feat_rows, node_rows)
    preact = summed + bias_vec.astype(jnp.float32)[:, None]
    activated, pullback = jax.vjp(smooth_gate, preact)
    grad_pre = pullback(cotangent.astype(jnp.float32))[0]
    grad_low = grad_pre.astype(jnp.bfloat16)
    grad_blocks = grad_low.reshape(feat_rows, blocks, tile_size)
    rows_picked = jnp.take(grad_blocks, tile_row, axis=1)
    backward = jnp.einsum(
        "ota,tab->otb", rows_picked, adj_tiles, preferred_element_type=jnp.float32
    )
    src_place = (tile_col[:, None] == jnp.arange(blocks + domains)[None, :]).astype(
        jnp.float32
    ) * live_float[:, None]
    recv_place = (send_block[:, None] == jnp.arange(blocks)[None, :]).astype(jnp.float32)
    own_sum = jnp.einsum(
        "otb,tr->orb", backward, src_place[:, :blocks], precision=lax.Precision.HIGHEST
    )
    slot_hit = jnp.logical_and(
        tile_col[:, None] == blocks + jnp.arange(domains)[None, :], live_tiles[:, None]
    )
    slot_rows = jnp.sum(jnp.where(slot_hit, tile_row[:, None], 0), axis=0)
    out_tiles = jnp.einsum(
        "tq,tab->qab", slot_hit.astype(jnp.bfloat16), adj_tiles, preferred_element_type=jnp.float32
    ).astype(jnp.bfloat16)
    out_rows = jnp.take(grad_blocks, slot_rows, axis=1)
    in_tiles = lax.all_to_all(out_tiles, "dom", split_axis=0, concat_axis=0, tiled=True)
    in_rows = lax.all_to_all(out_rows, "dom", split_axis=1, concat_axis=1, tiled=True)
    remote_sum = jnp.einsum("oqa,qab->oqb", in_rows, in_tiles, preferred_element_type=jnp.float32)
    grad_sum = own_sum + jnp.einsum(
        "oqb,qr->orb", remote_sum, recv_place, precision=lax.Precision.HIGHEST
    )
    grad_hidden = grad_sum.reshape(feat_rows, node_rows).astype(jnp.bfloat16)
    norm_scale = 1.0 / math.sqrt(domains * node_rows)
    weight_part = lax.dot_general(
        whole, grad_hidden, (((1,), (1,)), ((), ())), preferred_element_type=jnp.float32
    )
    bias_part = jnp.sum(grad_pre, axis=1)
    weight_sum, bias_sum = lax.psum((weight_part, bias_part), "dom")
    grad_weight = weight_sum * norm_scale
    grad_bias = bias_sum * norm_scale
    full_weight, all_grad = (
        lax.all_gather(weight, "feat", axis=1, tiled=True),
        lax.all_gather(grad_hidden, "feat", axis=0, tiled=True),
    )
    my_rows = lax.dynamic_slice_in_dim(
        full_weight, lax.axis_index("feat") * feat_rows, feat_rows, 0
    )
    grad_input = jnp.dot(my_rows, all_grad, preferred_element_type=jnp.float32).astype(jnp.bfloat16)
    return (activated.astype(jnp.bfloat16), grad_input, grad_weight, grad_bias)


def solution(mesh):
    placed = (
        P("feat", "dom"),
        P(None, "feat"),
        P("feat"),
        P("dom", None, None),
        P("dom"),
        P("dom"),
        P("dom"),
        P("dom"),
        P("feat", "dom"),
    )
    return jax.shard_map(
        per_device,
        mesh=mesh,
        in_specs=placed,
        out_specs=(P("feat", "dom"), P("feat", "dom"), P(None, "feat"), P("feat")),
        check_vma=False,
    )
```

profile of v0, /device:TPU:1, one launch (start us, length us, event | category | flops | bytes accessed | tf_op | source)
XLA Modules:
  0.0 581.7 jit_solution(17211733674106753430)
XLA Ops:
  7.2 0.7 all-gather.3.cloned.1.call-update
  7.9 0.9 compare_select_fusion.1
  9.4 34.6 %all-gather.3.cloned.1.call-done = bf16[256,2048]{1,0:T(8,128)(2,1)} async-done(((bf16[64,2048]{1,0:T(8,128)(2,1)}), bf16[256,2048]{1,0:T(8,128)(2,1)}) %all-gather.3.cloned.1.call-update) | async-done | bytes 1048592 | tf_op jit(solution)/shard_map/all_gather | solution.py:20
  44.0 1.5 fusion.23
  45.6 2.2 gather_fusion.2
  47.8 3.2 select_bitcast_fusion.1
  51.0 15.8 %all-to-all-start = ((bf16[64,128,128]{2,0,1:T(8,128)(2,1)}), bf16[64,128,128]{2,0,1:T(8,128)(2,1)}, u32[]{:S(2)}, u32[]{:S(2)}) async-start(bf16[64,128,128]{2,0,1:T(8,128)(2,1)} %select_bitcast_fusion.1), calls=%async_computation | async-start | bytes 4194304 | tf_op jit(solution)/shard_map/all_to_all | solution.py:26
  67.5 2.9 fusion.8
  70.4 4.7 copy.30
  75.1 42.6 %all-to-all-done = bf16[64,128,128]{2,0,1:T(8,128)(2,1)} async-done(((bf16[64,128,128]{2,0,1:T(8,128)(2,1)}), bf16[64,128,128]{2,0,1:T(8,128)(2,1)}, u32[]{:S(2)}, u32[]{:S(2)}) %all-to-all-start) | async-done | bytes 2097184 | tf_op jit(solution)/shard_map/all_to_all | solution.py:26
  117.7 9.3 %all-to-all-start.1 = ((bf16[128,128,128]{2,1,0:T(8,128)(2,1)}), bf16[128,128,128]{2,1,0:T(8,128)(2,1)}, u32[]{:S(2)}, u32[]{:S(2)}) async-start(bf16[128,128,128]{2,1,0:T(8,128)(2,1)} %copy.30), calls=%async_computation.1 | async-start | bytes 8388608 | tf_op jit(solution)/shard_map/all_to_all | solution.py:62
  127.3 3.3 pad_maximum_fusion
  130.6 3.6 gather_fusion
  134.2 3.6 convolution_bitcast_fusion.2
  137.8 3.3 fusion.6
  141.1 1.3 fusion.61
  142.6 2.1 gather_fusion.3
  144.7 3.2 select_bitcast_fusion
  147.9 75.7 %all-to-all-done.1 = bf16[128,128,128]{2,1,0:T(8,128)(2,1)} async-done(((bf16[128,128,128]{2,1,0:T(8,128)(2,1)}), bf16[128,128,128]{2,1,0:T(8,128)(2,1)}, u32[]{:S(2)}, u32[]{:S(2)}) %all-to-all-start.1) | async-done | bytes 4194336 | tf_op jit(solution)/shard_map/all_to_all | solution.py:62
  223.6 22.7 %all-to-all-start.2 = ((bf16[64,128,128]{2,0,1:T(8,128)(2,1)}), bf16[64,128,128]{2,0,1:T(8,128)(2,1)}, u32[]{:S(2)}, u32[]{:S(2)}) async-start(bf16[64,128,128]{2,0,1:T(8,128)(2,1)} %select_bitcast_fusion), calls=%async_computation.2 | async-start | bytes 4194304 | tf_op jit(solution)/shard_map/all_to_all | solution.py:63
  246.6 2.0 gather_fusion.1
  248.6 4.1 convolution_bitcast_fusion.1
  252.7 44.5 %all-to-all-done.2 = bf16[64,128,128]{2,0,1:T(8,128)(2,1)} async-done(((bf16[64,128,128]{2,0,1:T(8,128)(2,1)}), bf16[64,128,128]{2,0,1:T(8,128)(2,1)}, u32[]{:S(2)}, u32[]{:S(2)}) %all-to-all-start.2) | async-done | bytes 2097184 | tf_op jit(solution)/shard_map/all_to_all | solution.py:63
  297.2 4.0 convolution_bitcast_fusion
  301.3 3.8 fusion
  305.2 3.3 fusion.20
  308.5 1.1 convolution_bitcast_fusion.3
  309.6 0.8 copy.67
  310.4 9.1 %all_gather.10 = bf16[256,256]{0,1:T(8,128)(2,1)S(1)} all-gather(bf16[256,64]{0,1:T(8,128)(2,1)S(1)} %copy-done.4), channel_id=1, replica_groups=mesh['dom'=128,'feat'=4] {'feat'}, dimensions={1}, use_global_device_ids=true | all-gather | bytes 163840 | tf_op jit(solution)/shard_map/all_gather | solution.py:78
  319.5 251.3 %psum.15 = f32[64]{0:T(128)S(1)} all-reduce(f32[64]{0:T(128)S(1)} %get-tuple-element.5), channel_id=1, replica_groups=mesh['dom'=128,'feat'=4] {'dom'}, use_global_device_ids=true, to_apply=%region_3.5 | all-reduce | flops 64 | bytes 512 | tf_op jit(solution)/shard_map/psum | solution.py:74
  571.3 1.5 broadcast_multiply_fusion
  572.8 2.3 convolution_convert_fusion
  (44 shorter events, 1.9 us)
Async XLA Ops:
  7.2 60.3 %copy-start = (bf16[96,128,128]{2,1,0:T(8,128)(2,1)S(1)}, bf16[96,128,128]{2,1,0:T(8,128)(2,1)}, u32[]{:S(2)}) copy-start(bf16[96,128,128]{2,1,0:T(8,128)(2,1)} %param.14) | copy-start | bytes 9437188
  7.2 36.8 %all-gather.3.cloned.1.call-start = ((), (), s32[]{:S(2)}) async-start(), calls=%async_computation.3 | async-start | bytes 1310720 | tf_op jit(solution)/shard_map/all_gather | solution.py:20
  51.0 16.5 %copy-start.5 = (s32[96]{0:T(128)S(1)}, s32[96]{0:T(128)}, u32[]{:S(2)}) copy-start(s32[96]{0:T(128)} %param.16) | copy-start | bytes 1156
  51.0 66.7 %all-to-all-start = ((bf16[64,128,128]{2,0,1:T(8,128)(2,1)}), bf16[64,128,128]{2,0,1:T(8,128)(2,1)}, u32[]{:S(2)}, u32[]{:S(2)}) async-start(bf16[64,128,128]{2,0,1:T(8,128)(2,1)} %select_bitcast_fusion.1), calls=%async_computation | async-start | bytes 4194304 | tf_op jit(solution)/shard_map/all_to_all | solution.py:26
  75.1 52.0 %copy-start.8 = (bf16[64]{0:T(256)(128)(2,1)S(1)}, bf16[64]{0:T(256)(128)(2,1)}, u32[]{:S(2)}) copy-start(bf16[64]{0:T(256)(128)(2,1)} %param.13) | copy-start | bytes 388
  75.1 52.0 %copy-start.6 = (s32[96]{0:T(128)S(1)}, s32[96]{0:T(128)}, u32[]{:S(2)}) copy-start(s32[96]{0:T(128)} %param.15) | copy-start | bytes 1156
  117.7 105.8 %all-to-all-start.1 = ((bf16[128,128,128]{2,1,0:T(8,128)(2,1)}), bf16[128,128,128]{2,1,0:T(8,128)(2,1)}, u32[]{:S(2)}, u32[]{:S(2)}) async-start(bf16[128,128,128]{2,1,0:T(8,128)(2,1)} %copy.30), calls=%async_computation.1 | async-start | bytes 8388608 | tf_op jit(solution)/shard_map/all_to_all | solution.py:62
  137.8 3.3 copy-start.3
  223.6 73.6 %all-to-all-start.2 = ((bf16[64,128,128]{2,0,1:T(8,128)(2,1)}), bf16[64,128,128]{2,0,1:T(8,128)(2,1)}, u32[]{:S(2)}, u32[]{:S(2)}) async-start(bf16[64,128,128]{2,0,1:T(8,128)(2,1)} %select_bitcast_fusion), calls=%async_computation.2 | async-start | bytes 4194304 | tf_op jit(solution)/shard_map/all_to_all | solution.py:63
  246.3 325.0 %all-reduce.2.cloned.1.call-start = ((), (), s32[]{:S(2)}) async-start(), calls=%async_computation.5 | async-start | bytes 131072 | tf_op jit(solution)/shard_map/psum | solution.py:74
  252.7 48.5 %copy-start.7 = (s32[128]{0:T(128)S(1)}, s32[128]{0:T(128)}, u32[]{:S(2)}) copy-start(s32[128]{0:T(128)} %param.18) | copy-start | bytes 1540
  301.3 3.9 copy-start.1
  305.1 3.3 copy-start.2
  305.1 5.3 copy-start.4
  309.6 263.2 %all-gather.5.cloned.1.call-start = ((), (), s32[]{:S(2)}) async-start(), calls=%async_computation.4 | async-start | bytes 1310720 | tf_op jit(solution)/shard_map/all_gather | solution.py:79
Sparse Core Ops, SparseCore 0:
  10.1 33.8 all-gather.2
  309.7 175.5 all-reduce.1
  488.0 21.2 all-gather.4
where the time goes:
time: 582 us
  blocking collectives  260 us (45%)
  waiting for transfers between devices  198 us (34%)
  starting transfers between devices  48.1 us (8%)
  matrix products  30.1 us (5%)
  local copies, waits for them, and re-layouts  15.6 us (3%)
  other arithmetic  14.7 us (3%)
  between operations  14.7 us (3%)
    psum x1, blocking collectives, per_device(): weight_sum, bias_sum = lax.psum((weight_part, bias_part), 'dom')  251 us
    all_to_all x1, waiting for transfers between devices, per_device(): lax.all_to_all(out_tiles, 'dom', split_axis=0, concat_axis=0, tiled=True)  75.7 us
    all_to_all x1, waiting for transfers between devices, per_device(): lax.all_to_all(out_rows, 'dom', split_axis=1, concat_axis=1, tiled=True)  44.5 us
    all_to_all x1, waiting for transfers between devices, per_device(): lax.all_to_all(outgoing, 'dom', split_axis=1, concat_axis=1, tiled=True)  42.6 us
    all_gather x1, waiting for transfers between devices, per_device(): whole = lax.all_gather(node_feats, 'feat', axis=0, tiled=True)  34.6 us
    all_to_all x1, starting transfers between devices, per_device(): lax.all_to_all(out_rows, 'dom', split_axis=1, concat_axis=1, tiled=True)  22.7 us
    all_to_all x1, starting transfers between devices, per_device(): lax.all_to_all(outgoing, 'dom', split_axis=1, concat_axis=1, tiled=True)  15.8 us
  transfers between devices with their start and end apart: 6, of which 4 were waited for; matrix products, arithmetic and copies ran while one was open for 7% of the time, Pallas kernels for 0%

commit v1 on v0

--- a/solution.py
+++ b/solution.py
@@ -60,7 +60,10 @@
     ).astype(jnp.bfloat16)
     out_rows = jnp.take(grad_blocks, slot_rows, axis=1)
     in_tiles = lax.all_to_all(out_tiles, "dom", split_axis=0, concat_axis=0, tiled=True)
-    in_rows = lax.all_to_all(out_rows, "dom", split_axis=1, concat_axis=1, tiled=True)
+    in_rows = jnp.concatenate(
+        lax.all_to_all(jnp.stack(jnp.split(out_rows, lax.axis_size("dom"), axis=1)), "dom", 0, 0),
+        axis=1,
+    )
     remote_sum = jnp.einsum("oqa,qab->oqb", in_rows, in_tiles, preferred_element_type=jnp.float32)
     grad_sum = own_sum + jnp.einsum(
         "oqb,qr->orb", remote_sum, recv_place, precision=lax.Precision.HIGHEST

time: 582 us -> 579 us (level)
  local copies, waits for them, and re-layouts: 15.6 us -> 92.5 us
  waiting for transfers between devices: 198 us -> 123 us
    unnamed x19 -> x146, local copies, waits for them, and re-layouts: 0.82 us -> 77 us
    all_to_all x1, waiting for transfers between devices: 75.7 us -> 0.62 us  [per_device(): lax.all_to_all(out_tiles, 'dom', split_axis=0, concat_axis=0, tiled=True)]
  transfers between devices with their start and end apart: 6 -> 6, of which waited for: 4 -> 4; matrix products, arithmetic and copies ran while one was open for 7% -> 20% of each run, Pallas kernels for 0% -> 0%
where the time goes in v1:
time: 579 us; the launch traced here: 578 us
  blocking collectives  260 us (45%)
  waiting for transfers between devices  123 us (21%)
  local copies, waits for them, and re-layouts  92.5 us (16%)
  starting transfers between devices  44.6 us (8%)
  matrix products  30.1 us (5%)
  between operations  14.7 us (3%)
  other arithmetic  13.4 us (2%)
    psum x1, blocking collectives, per_device(): weight_sum, bias_sum = lax.psum((weight_part, bias_part), 'dom')  251 us
    unnamed x146, local copies, waits for them, and re-layouts  77 us
    all_to_all x1, waiting for transfers between devices, per_device(): lax.all_to_all(jnp.stack(jnp.split(out_rows, lax.axis_size('dom'), axis=1...  44.5 us
    all_to_all x1, waiting for transfers between devices, per_device(): lax.all_to_all(outgoing, 'dom', split_axis=1, concat_axis=1, tiled=True)  42.4 us
    all_gather x1, waiting for transfers between devices, per_device(): whole = lax.all_gather(node_feats, 'feat', axis=0, tiled=True)  34.6 us
    all_to_all x1, starting transfers between devices, per_device(): lax.all_to_all(jnp.stack(jnp.split(out_rows, lax.axis_size('dom'), axis=1...  19.1 us
    all_to_all x1, starting transfers between devices, per_device(): lax.all_to_all(outgoing, 'dom', split_axis=1, concat_axis=1, tiled=True)  15.8 us
  transfers between devices with their start and end apart: 6, of which 4 were waited for; matrix products, arithmetic and copies ran while one was open for 20% of the time, Pallas kernels for 0%

profile of v1, /device:TPU:1, one launch (start us, length us, event | category | flops | bytes accessed | tf_op | source)
XLA Modules:
  0.0 578.4 jit_solution(15382521956957447353)
XLA Ops:
  7.2 0.7 all-gather.3.cloned.1.call-update
  7.9 0.9 compare_select_fusion.1
  8.8 0.7 compare_and_fusion.3
  9.4 34.6 %all-gather.3.cloned.1.call-done = bf16[256,2048]{1,0:T(8,128)(2,1)} async-done(((bf16[64,2048]{1,0:T(8,128)(2,1)}), bf16[256,2048]{1,0:T(8,128)(2,1)}) %all-gather.3.cloned.1.call-update) | async-done | bytes 1048592 | tf_op jit(solution)/shard_map/all_gather | solution.py:20
  44.0 1.5 fusion.24
  45.6 2.2 gather_fusion.2
  47.8 3.2 select_bitcast_fusion.1
  51.1 15.8 %all-to-all-start = ((bf16[64,128,128]{2,0,1:T(8,128)(2,1)}), bf16[64,128,128]{2,0,1:T(8,128)(2,1)}, u32[]{:S(2)}, u32[]{:S(2)}) async-start(bf16[64,128,128]{2,0,1:T(8,128)(2,1)} %select_bitcast_fusion.1), calls=%async_computation | async-start | bytes 4194304 | tf_op jit(solution)/shard_map/all_to_all | solution.py:26
  67.6 2.9 fusion.8
  70.5 4.7 copy.284
  75.4 42.4 %all-to-all-done = bf16[64,128,128]{2,0,1:T(8,128)(2,1)} async-done(((bf16[64,128,128]{2,0,1:T(8,128)(2,1)}), bf16[64,128,128]{2,0,1:T(8,128)(2,1)}, u32[]{:S(2)}, u32[]{:S(2)}) %all-to-all-start) | async-done | bytes 2097184 | tf_op jit(solution)/shard_map/all_to_all | solution.py:26
  117.8 9.3 %all-to-all-start.1 = ((bf16[128,128,128]{2,1,0:T(8,128)(2,1)}), bf16[128,128,128]{2,1,0:T(8,128)(2,1)}, u32[]{:S(2)}, u32[]{:S(2)}) async-start(bf16[128,128,128]{2,1,0:T(8,128)(2,1)} %copy.284), calls=%async_computation.1 | async-start | bytes 8388608 | tf_op jit(solution)/shard_map/all_to_all | solution.py:62
  127.1 3.3 pad_maximum_fusion
  130.4 3.6 gather_fusion
  134.0 3.6 convolution_bitcast_fusion.2
  137.6 3.3 fusion.6
  140.9 1.4 fusion.61
  142.4 2.2 gather_fusion.3
  144.6 1.9 select_bitcast_fusion
  223.9 19.1 %all-to-all-start.2 = ((bf16[128,64,1,128]{3,1,2,0:T(8,128)(2,1)}), bf16[128,64,1,128]{3,1,2,0:T(8,128)(2,1)}, u32[]{:S(2)}, u32[]{:S(2)}) async-start(bf16[128,64,1,128]{3,1,2,0:T(8,128)(2,1)} %constant_dynamic-update-slice_fusion), calls=%async_computation.2 | async-start | bytes 4194304 | tf_op jit(solution)/shard_map/all_to_all | solution.py:64
  243.3 2.0 gather_fusion.1
  245.4 4.1 convolution_bitcast_fusion.1
  249.5 44.5 %all-to-all-done.2 = bf16[128,64,1,128]{3,1,2,0:T(8,128)(2,1)} async-done(((bf16[128,64,1,128]{3,1,2,0:T(8,128)(2,1)}), bf16[128,64,1,128]{3,1,2,0:T(8,128)(2,1)}, u32[]{:S(2)}, u32[]{:S(2)}) %all-to-all-start.2) | async-done | bytes 2097184 | tf_op jit(solution)/shard_map/all_to_all | solution.py:64
  294.0 4.0 convolution_bitcast_fusion
  298.0 3.8 fusion
  301.9 3.3 fusion.21
  305.2 1.1 convolution_bitcast_fusion.3
  306.4 0.8 copy.322
  307.2 9.1 %all_gather.10 = bf16[256,256]{0,1:T(8,128)(2,1)S(1)} all-gather(bf16[256,64]{0,1:T(8,128)(2,1)S(1)} %copy-done.4), channel_id=1, replica_groups=mesh['dom'=128,'feat'=4] {'feat'}, dimensions={1}, use_global_device_ids=true | all-gather | bytes 163840 | tf_op jit(solution)/shard_map/all_gather | solution.py:81
  316.3 251.3 %psum.15 = f32[64]{0:T(128)S(1)} all-reduce(f32[64]{0:T(128)S(1)} %get-tuple-element.5), channel_id=1, replica_groups=mesh['dom'=128,'feat'=4] {'dom'}, use_global_device_ids=true, to_apply=%region_3.5 | all-reduce | flops 64 | bytes 512 | tf_op jit(solution)/shard_map/psum | solution.py:77
  568.0 1.5 broadcast_multiply_fusion
  569.5 2.3 convolution_convert_fusion
  (171 shorter events, 78.7 us)
Async XLA Ops:
  7.2 60.4 %copy-start = (bf16[96,128,128]{2,1,0:T(8,128)(2,1)S(1)}, bf16[96,128,128]{2,1,0:T(8,128)(2,1)}, u32[]{:S(2)}) copy-start(bf16[96,128,128]{2,1,0:T(8,128)(2,1)} %param.14) | copy-start | bytes 9437188
  7.2 36.8 %all-gather.3.cloned.1.call-start = ((), (), s32[]{:S(2)}) async-start(), calls=%async_computation.3 | async-start | bytes 1310720 | tf_op jit(solution)/shard_map/all_gather | solution.py:20
  51.1 15.8 %copy-start.8 = (bf16[64]{0:T(256)(128)(2,1)S(1)}, bf16[64]{0:T(256)(128)(2,1)}, u32[]{:S(2)}) copy-start(bf16[64]{0:T(256)(128)(2,1)} %param.13) | copy-start | bytes 388
  51.1 16.5 %copy-start.5 = (s32[96]{0:T(128)S(1)}, s32[96]{0:T(128)}, u32[]{:S(2)}) copy-start(s32[96]{0:T(128)} %param.16) | copy-start | bytes 1156
  51.1 66.7 %all-to-all-start = ((bf16[64,128,128]{2,0,1:T(8,128)(2,1)}), bf16[64,128,128]{2,0,1:T(8,128)(2,1)}, u32[]{:S(2)}, u32[]{:S(2)}) async-start(bf16[64,128,128]{2,0,1:T(8,128)(2,1)} %select_bitcast_fusion.1), calls=%async_computation | async-start | bytes 4194304 | tf_op jit(solution)/shard_map/all_to_all | solution.py:26
  70.5 4.7 copy-start.6
  117.8 106.2 %all-to-all-start.1 = ((bf16[128,128,128]{2,1,0:T(8,128)(2,1)}), bf16[128,128,128]{2,1,0:T(8,128)(2,1)}, u32[]{:S(2)}, u32[]{:S(2)}) async-start(bf16[128,128,128]{2,1,0:T(8,128)(2,1)} %copy.284), calls=%async_computation.1 | async-start | bytes 8388608 | tf_op jit(solution)/shard_map/all_to_all | solution.py:62
  137.6 3.3 copy-start.3
  223.9 70.0 %all-to-all-start.2 = ((bf16[128,64,1,128]{3,1,2,0:T(8,128)(2,1)}), bf16[128,64,1,128]{3,1,2,0:T(8,128)(2,1)}, u32[]{:S(2)}, u32[]{:S(2)}) async-start(bf16[128,64,1,128]{3,1,2,0:T(8,128)(2,1)} %constant_dynamic-update-slice_fusion), calls=%async_computation.2 | async-start | bytes 4194304 | tf_op jit(solution)/shard_map/all_to_all | solution.py:64
  243.0 325.0 %all-reduce.2.cloned.1.call-start = ((), (), s32[]{:S(2)}) async-start(), calls=%async_computation.5 | async-start | bytes 131072 | tf_op jit(solution)/shard_map/psum | solution.py:77
  249.5 48.5 %copy-start.7 = (s32[128]{0:T(128)S(1)}, s32[128]{0:T(128)}, u32[]{:S(2)}) copy-start(s32[128]{0:T(128)} %param.18) | copy-start | bytes 1540
  298.0 3.9 copy-start.1
  301.9 3.3 copy-start.2
  305.2 2.0 copy-start.4
  306.3 263.2 %all-gather.5.cloned.1.call-start = ((), (), s32[]{:S(2)}) async-start(), calls=%async_computation.4 | async-start | bytes 1310720 | tf_op jit(solution)/shard_map/all_gather | solution.py:82
Sparse Core Ops, SparseCore 0:
  10.1 33.8 all-gather.2
  306.4 175.5 all-reduce.1
  484.7 21.2 all-gather.4
